TPU v7x, 32 devices: a whole 2x2x4 slice. The times are simulated.
32 devices in a mesh: seq: 8 (over y, x, core), tp: 4 (over z).
Axes of the slice: x: 2, y: 2, z: 4, core: 2. Of those that a mesh axis runs over, the one named last changes fastest.
Arguments:
- hidden: bfloat16 [4096, 2560], P('seq', 'tp'), may hold values from -6 to 6
- norm_gain: float32 [2560], replicated, may hold values from 0.25 to 1.75
- query_weight: float32 [2560, 4096], P('seq', 'tp'), may hold values from -0.125 to 0.125
- key_weight: float32 [2560, 1024], P('seq', 'tp'), may hold values from -0.125 to 0.125
- value_weight: float32 [2560, 1024], P('seq', 'tp'), may hold values from -0.125 to 0.125
- query_gain: float32 [128], replicated, may hold values from 0.5 to 8
- key_gain: float32 [128], replicated, may hold values from 0.5 to 8
- lengths: int32 [8], replicated, may hold values from 1 to 2048, 4096 in all
- page_table: int32 [32], replicated, may hold values from 0 to 31, each once
Outputs:
- attention: bfloat16 [4096, 4096], P('seq', 'tp')
- key_cache: bfloat16 [32, 8, 128, 128], P('seq', 'tp')
- value_cache: bfloat16 [32, 8, 128, 128], P('seq', 'tp')
Inputs may be any that keep to these rules, and one draw needn't show every extreme that they name: 8 positive lengths summing to 4096; the longest is exactly 2048. `page_table`: every page is named by exactly one block.
All inputs are finite; a program needn't handle non-finite values.
Results may differ from a plain program's by a relative error of at most 0.0085.
The roundings to bfloat16 on the way count: a program that leaves them out, or rounds other values in their place, can miss the bound.
Values may be sent and summed in bfloat16 or wider, within the bound.
No kernel may reach another device: no remote copies, remote signals or barrier semaphores. Data moves between devices by JAX's collectives and lax.ppermute only.
A program may use at most 128 MiB of HBM per device.

v0:
```python
from functools import partial
import jax
import jax.numpy as jnp
from jax import lax
from jax.sharding import PartitionSpec as P

PAGE = 128
epsilon = 1e-06
excluded = -1e30


def segment_of(slot_index, prompt_ends):
    return jnp.sum((slot_index[..., None] >= prompt_ends).astype(jnp.int32), axis=-1)


def position_of(slot_index, prompt_ends, lengths):
    segment_id = segment_of(slot_index, prompt_ends)
    prompt_starts = prompt_ends - lengths
    labels = jnp.arange(lengths.shape[0], dtype=jnp.int32)
    picked = jnp.sum(jnp.where(segment_id[..., None] == labels, prompt_starts, 0), axis=-1)
    return (segment_id, slot_index - picked)


def head_norm(vectors, gain):
    mean_sq = jnp.mean(vectors * vectors, axis=-1, keepdims=True)
    return vectors * lax.rsqrt(mean_sq + epsilon) * gain


def rotate(vectors, position):
    head_dim = vectors.shape[-1]
    half_dim = head_dim // 2
    frequency = 1000000.0 ** (-(jnp.arange(half_dim, dtype=jnp.float32) * 2.0 / head_dim))
    angles = position.astype(jnp.float32)[:, None] * frequency[None, :]
    cosine = jnp.cos(angles)[:, None, :]
    sine_part = jnp.sin(angles)[:, None, :]
    front = vectors[..., :half_dim]
    back_half = vectors[..., half_dim:]
    return jnp.concatenate(
        [front * cosine - back_half * sine_part, back_half * cosine + front * sine_part], axis=-1
    )


def attend(
    query_block,
    query_slots,
    query_segments,
    key_piece,
    value_piece,
    key_slots,
    key_segments,
    kv_heads,
    group_size,
    head_dim,
    running,
):
    running_max, denominator, accumulator = running
    half_rows = query_block.shape[0]
    key_count = key_piece.shape[0]
    scores = jnp.einsum(
        "qkgd,nkd->kgqn",
        query_block.reshape(half_rows, kv_heads, group_size, head_dim),
        key_piece.reshape(key_count, kv_heads, head_dim),
        preferred_element_type=jnp.float32,
    ) * head_dim ** (-0.5)
    allowed = (key_segments[None, :] == query_segments[:, None]) & (
        key_slots[None, :] <= query_slots[:, None]
    )
    masked = jnp.where(allowed, scores, excluded)
    new_max = jnp.maximum(running_max, jnp.max(masked, axis=-1))
    weights = jnp.where(allowed, jnp.exp(scores - new_max[..., None]), 0.0)
    denominator = jnp.sum(weights, axis=-1)
    probs = weights.astype(jnp.bfloat16)
    accumulator = jnp.einsum(
        "kgqn,nkd->kgqd",
        probs,
        value_piece.reshape(key_count, kv_heads, head_dim),
        preferred_element_type=jnp.float32,
    )
    return (new_max, denominator, accumulator)


def keep_state(running):
    return running


def shards(
    hidden,
    norm_gain,
    query_weight,
    key_weight,
    value_weight,
    query_gain,
    key_gain,
    lengths,
    page_table,
):
    row_count = hidden.shape[0]
    half_rows = row_count // 2
    head_dim = query_gain.shape[0]
    query_cols = query_weight.shape[1]
    key_cols = key_weight.shape[1]
    kv_heads = key_cols // head_dim
    group_size = query_cols // key_cols
    seq_rank = lax.axis_index("seq")
    prompt_ends = jnp.cumsum(lengths)
    gathered = lax.all_gather(hidden, "tp", axis=1, tiled=True)
    widened = gathered.astype(jnp.float32)
    normed = (
        widened
        * lax.rsqrt(jnp.mean(widened * widened, axis=-1, keepdims=True) + epsilon)
        * norm_gain
    ).astype(jnp.bfloat16)
    server_block = jnp.concatenate([query_weight, key_weight, value_weight], axis=1).astype(
        jnp.bfloat16
    )
    projected = jnp.dot(
        normed,
        lax.all_gather(server_block, "seq", axis=0, tiled=True),
        preferred_element_type=jnp.float32,
    )
    slot_index = seq_rank * row_count + jnp.arange(row_count, dtype=jnp.int32)
    segment_id, position = position_of(slot_index, prompt_ends, lengths)
    queries = rotate(
        head_norm(
            projected[:, :query_cols].reshape(row_count, query_cols // head_dim, head_dim),
            query_gain,
        ),
        position,
    )
    queries = queries.reshape(row_count, query_cols).astype(jnp.bfloat16)
    key_rows = rotate(
        head_norm(
            projected[:, query_cols : query_cols + key_cols].reshape(row_count, kv_heads, head_dim),
            key_gain,
        ),
        position,
    )
    key_rows = key_rows.reshape(row_count, key_cols).astype(jnp.bfloat16)
    values = projected[:, query_cols + key_cols :].astype(jnp.bfloat16)
    shipped = queries[half_rows:]
    other_slots = slot_index[half_rows:]
    query_blocks = (queries[:half_rows], shipped)
    block_slots = (slot_index[:half_rows], other_slots)
    block_segments = (
        segment_of(block_slots[0], prompt_ends),
        segment_of(block_slots[1], prompt_ends),
    )
    pages_dev = row_count // PAGE
    owned_pages = seq_rank * pages_dev + jnp.arange(pages_dev, dtype=jnp.int32)
    page_count = page_table.shape[0]
    source_block = jnp.sum(
        jnp.where(
            page_table[None, :] == owned_pages[:, None],
            jnp.arange(page_count, dtype=jnp.int32)[None, :],
            0,
        ),
        axis=1,
    )

    def empty_state():
        return (
            jnp.full((kv_heads, group_size, half_rows), excluded, jnp.float32),
            jnp.zeros((kv_heads, group_size, half_rows), jnp.float32),
            jnp.zeros((kv_heads, group_size, half_rows, head_dim), jnp.float32),
        )

    empty_pages = jnp.zeros((pages_dev, PAGE, key_cols), jnp.bfloat16)
    initial = (empty_state(), empty_state(), empty_pages, empty_pages)
    first_row = jnp.int32(0)
    key_piece = lax.all_gather(key_rows, "seq", axis=0, tiled=True)
    value_piece = lax.all_gather(values, "seq", axis=0, tiled=True)
    key_count = key_piece.shape[0]
    key_slots = jnp.arange(key_count, dtype=jnp.int32)
    key_segments = segment_of(key_slots, prompt_ends)
    states = []
    for fold_half_number in range(2):
        query_slots = block_slots[fold_half_number]
        query_segments = block_segments[fold_half_number]
        last_query = query_slots[-1]
        clipped = jnp.minimum(first_row + key_count - 1, last_query)
        is_live = (first_row <= last_query) & (
            segment_of(clipped, prompt_ends) >= query_segments[0]
        )
        update = partial(
            attend,
            query_blocks[fold_half_number],
            query_slots,
            query_segments,
            key_piece,
            value_piece,
            key_slots,
            key_segments,
            kv_heads,
            group_size,
            head_dim,
        )
        states.append(lax.cond(is_live, update, keep_state, initial[fold_half_number]))
    blocks_in = key_count // PAGE
    block_number = jnp.arange(blocks_in, dtype=jnp.int32)
    matches = source_block[:, None] == block_number[None, :]
    selector = matches.astype(jnp.bfloat16)
    has_page = jnp.any(matches, axis=1)[:, None, None]
    new_keys = jnp.einsum(
        "pj,jtc->ptc",
        selector,
        key_piece.reshape(blocks_in, PAGE, key_cols),
        preferred_element_type=jnp.float32,
    ).astype(jnp.bfloat16)
    new_values = jnp.einsum(
        "pj,jtc->ptc",
        selector,
        value_piece.reshape(blocks_in, PAGE, key_cols),
        preferred_element_type=jnp.float32,
    ).astype(jnp.bfloat16)
    key_pages = jnp.where(has_page, new_keys, initial[2])
    value_pages = jnp.where(has_page, new_values, initial[3])
    result = (states[0], states[1], key_pages, value_pages)
    outputs = []
    for half_number in range(2):
        running_max, denominator, accumulator = result[half_number]
        result_block = accumulator / denominator[..., None]
        outputs.append(
            result_block.transpose(2, 0, 1, 3).reshape(half_rows, query_cols).astype(jnp.bfloat16)
        )
    returned = outputs[1]
    attention = jnp.concatenate([outputs[0], returned], axis=0)
    key_cache = result[2].reshape(pages_dev, PAGE, kv_heads, head_dim).transpose(0, 2, 1, 3)
    value_cache = result[3].reshape(pages_dev, PAGE, kv_heads, head_dim).transpose(0, 2, 1, 3)
    return (attention, key_cache, value_cache)


def solution(mesh):
    return jax.shard_map(
        shards,
        mesh=mesh,
        in_specs=(
            P("seq", "tp"),
            P(),
            P("seq", "tp"),
            P("seq", "tp"),
            P("seq", "tp"),
            P(),
            P(),
            P(),
            P(),
        ),
        out_specs=(P("seq", "tp"), P("seq", "tp", None, None), P("seq", "tp", None, None)),
        check_vma=False,
    )
```

profile of v0, /device:TPU:0, one launch (start us, length us, event | category | flops | bytes accessed | tf_op | source)
XLA Modules:
  0.0 328.1 jit_solution(12261171779500501294)
XLA Ops:
  15.4 1.8 multiply_cosine_fusion
  17.2 49.7 %all-gather.5.cloned.1.call-done = bf16[512,2560]{1,0:T(8,128)(2,1)} async-done(((bf16[512,640]{1,0:T(8,128)(2,1)}), bf16[512,2560]{1,0:T(8,128)(2,1)}) %all-gather.5.cloned.1.call-update) | async-done | bytes 2621456 | tf_op jit(solution)/shard_map/all_gather | solution.py:106
  66.9 2.3 fusion.26
  69.3 50.9 %all-gather.7.cloned.1.call-done = bf16[2560,1536]{1,0:T(8,128)(2,1)} async-done(((bf16[320,1536]{1,0:T(8,128)(2,1)}), bf16[2560,1536]{1,0:T(8,128)(2,1)}) %all-gather.7.cloned.1.call-update) | async-done | bytes 7864336 | tf_op jit(solution)/shard_map/all_gather | solution.py:118
  120.1 7.5 %fusion.29 = f32[512,1536]{1,0:T(8,128)S(1)} fusion(bf16[2560,1536]{1,0:T(8,128)(2,1)} %all-gather.7.cloned.1.call-done, bf16[512,2560]{1,0:T(8,128)(2,1)} %all-gather.5.cloned.1.call-done, f32[2560]{0:T(1024)S(1)} %copy-done.11, f32[512]{0:T(512)S(1)} %add_rsqrt_fusion.2), kind=kOutput, calls=%fused_computation.37 | convolution fusion | flops 4031774720 | bytes 13643776 | tf_op jit(solution)/shard_map/dot_general | solution.py:116
  132.8 1.9 subtract_convert_fusion.1
  136.3 1.8 slice.80
  149.0 15.2 %all-gather.9.cloned.1.call-done = bf16[4096,256]{1,0:T(8,128)(2,1)} async-done(((bf16[512,256]{1,0:T(8,128)(2,1)}), bf16[4096,256]{1,0:T(8,128)(2,1)}) %all-gather.9.cloned.1.call-update) | async-done | bytes 2097168 | tf_op jit(solution)/shard_map/all_gather | solution.py:170
  164.2 29.6 %all-gather.11.cloned.1.call-done = bf16[4096,256]{1,0:T(8,128)(2,1)} async-done(((bf16[512,256]{1,0:T(8,128)(2,1)}), bf16[4096,256]{1,0:T(8,128)(2,1)}) %all-gather.11.cloned.1.call-update) | async-done | bytes 2097168 | tf_op jit(solution)/shard_map/all_gather | solution.py:171
  193.7 55.7 %conditional.2 = (f32[2,4,256]{2,1,0:T(4,128)S(1)}, f32[2,4,256,128]{3,2,1,0:T(8,128)}) conditional(s32[]{:T(128)} %convert_element_type.81, () %tuple.24, (s32[4096]{0:T(1024)S(1)}, s32[256]{0:T(256)S(1)}, s32[4096]{0:T(1024)S(1)}, s32[256]{0:T(256)S(1)}, bf16[4096,256]{1,0:T(8,128)(2,1)}, /*index=5*/bf16[512,1024]{0,1:T(8,128)(2,1)}, ...), branch_computations={%region_9.10_spmd, %region_10.13_spmd} | conditional | flops 4390385664 | bytes 128534568 | solution.py:197
  195.1 4.0 %reshape.185 = bf16[4096,2,128]{2,1,0:T(2,128)(2,1)} reshape(bf16[4096,256]{1,0:T(8,128)(2,1)} %get-tuple-element.34) | data formatting | bytes 4194304 | tf_op jit(solution)/shard_map/cond/branch_1_fun/reshape | solution.py:62
  200.2 15.4 %fusion = (f32[2,4,256]{2,1,0:T(4,128)S(1)}, f32[2,4096,256,4]{2,1,3,0:T(8,128)}) fusion(pred[256,4096]{0,1:T(8,128)(4,1)S(1)} %compare_and_fusion, bf16[256,2,4,128]{0,3,2,1:T(8,128)(2,1)S(1)} %bitcast.84, bf16[4096,2,128,1]{2,1,0,3:T(2,128)(2,1)} %bitcast.78), kind=kOutput, calls=%fused_computation.2 | convolution fusion | flops 2172647424 | bytes 37232640 | tf_op jit(solution)/shard_map/cond/branch_1_fun/qkgd,nkd->kgqn/dot_general | solution.py:59
  215.6 2.0 reshape.187
  217.6 17.5 %fusion.5 = f32[2,4,256,128]{3,2,1,0:T(8,128)} fusion(f32[2,4096,256,4]{2,1,3,0:T(8,128)} %get-tuple-element.60, f32[2,4,256]{2,1,0:T(4,128)S(1)} %broadcast_maximum_fusion, pred[256,4096]{0,1:T(8,128)(4,1)S(1)} %compare_and_fusion, bf16[4096,2,128,1]{2,1,0,3:T(2,128)(2,1)} %bitcast.80), kind=kOutput, calls=%fused_computation.7 | convolution fusion | flops 2181038080 | bytes 37756928 | tf_op jit(solution)/shard_map/cond/branch_1_fun/kgqn,nkd->kgqd/dot_general | solution.py:73
  235.1 14.3 %fusion.4 = f32[2,4,256]{2,1,0:T(4,128)S(1)} fusion(f32[2,4096,256,4]{2,1,3,0:T(8,128)} %get-tuple-element.60, f32[2,4,256]{2,1,0:T(4,128)S(1)} %broadcast_maximum_fusion, pred[256,4096]{0,1:T(8,128)(4,1)S(1)} %compare_and_fusion), kind=kLoop, calls=%fused_computation.6 | loop fusion | flops 33552384 | bytes 34619392 | tf_op jit(solution)/shard_map/cond/branch_1_fun/reduce_sum | solution.py:71
  252.6 56.0 %conditional.3 = (f32[2,4,256]{2,1,0:T(4,128)S(1)}, f32[2,4,256,128]{3,2,1,0:T(8,128)}) conditional(s32[]{:T(128)} %convert_element_type.94, () %tuple.26, (s32[4096]{0:T(1024)S(1)}, s32[256]{0:T(256)S(1)}, s32[4096]{0:T(1024)S(1)}, s32[256]{0:T(256)S(1)}, bf16[4096,256]{1,0:T(8,128)(2,1)}, /*index=5*/bf16[512,1024]{0,1:T(8,128)(2,1)}, ...), branch_computations={%region_15.16_spmd, %region_16.19_spmd} | conditional | flops 4390385664 | bytes 128534568 | solution.py:197
  254.0 4.0 %reshape.188 = bf16[4096,2,128]{2,1,0:T(2,128)(2,1)} reshape(bf16[4096,256]{1,0:T(8,128)(2,1)} %get-tuple-element.41) | data formatting | bytes 4194304 | tf_op jit(solution)/shard_map/cond/branch_1_fun/reshape | solution.py:62
  259.0 15.4 %fusion.13 = (f32[2,4,256]{2,1,0:T(4,128)S(1)}, f32[2,4096,256,4]{2,1,3,0:T(8,128)}) fusion(pred[256,4096]{0,1:T(8,128)(4,1)S(1)} %compare_and_fusion.1, bf16[256,2,4,128]{0,3,2,1:T(8,128)(2,1)S(1)} %bitcast.85, bf16[4096,2,128,1]{2,1,0,3:T(2,128)(2,1)} %bitcast.79), kind=kOutput, calls=%fused_computation.18 | convolution fusion | flops 2172647424 | bytes 37232640 | tf_op jit(solution)/shard_map/cond/branch_1_fun/qkgd,nkd->kgqn/dot_general | solution.py:59
  274.4 2.0 reshape.190
  276.5 17.5 %fusion.18 = f32[2,4,256,128]{3,2,1,0:T(8,128)} fusion(f32[2,4096,256,4]{2,1,3,0:T(8,128)} %get-tuple-element.62, f32[2,4,256]{2,1,0:T(4,128)S(1)} %broadcast_maximum_fusion.1, pred[256,4096]{0,1:T(8,128)(4,1)S(1)} %compare_and_fusion.1, bf16[4096,2,128,1]{2,1,0,3:T(2,128)(2,1)} %bitcast.81), kind=kOutput, calls=%fused_computation.23 | convolution fusion | flops 2181038080 | bytes 37756928 | tf_op jit(solution)/shard_map/cond/branch_1_fun/kgqn,nkd->kgqd/dot_general | solution.py:73
  293.9 14.3 %fusion.17 = f32[2,4,256]{2,1,0:T(4,128)S(1)} fusion(f32[2,4096,256,4]{2,1,3,0:T(8,128)} %get-tuple-element.62, f32[2,4,256]{2,1,0:T(4,128)S(1)} %broadcast_maximum_fusion.1, pred[256,4096]{0,1:T(8,128)(4,1)S(1)} %compare_and_fusion.1), kind=kLoop, calls=%fused_computation.22 | loop fusion | flops 33552384 | bytes 34619392 | tf_op jit(solution)/shard_map/cond/branch_1_fun/reduce_sum | solution.py:71
  308.5 1.7 fusion.50
  311.8 3.6 %fusion.46 = bf16[4,128,256]{2,0,1:T(4,128)(2,1)} fusion(bf16[32,128,256]{2,1,0:T(8,128)(2,1)} %bitcast.76, pred[4]{0:T(512)(128)(4,1)S(1)} %fusion.52, s32[4]{0:T(128)S(1)} %select_reduce_fusion.1), kind=kOutput, calls=%fused_computation.52 | convolution fusion | flops 8650880 | bytes 2359316 | tf_op jit(solution)/shard_map/pj,jtc->ptc/dot_general | solution.py:203
  316.5 2.0 fusion.43
  (89 shorter events, 34.3 us)
Async XLA Ops:
  7.2 7.2 %copy-start.10 = (s32[8]{0:T(128)S(1)}, s32[8]{0:T(128)}, u32[]{:S(2)}) copy-start(s32[8]{0:T(128)} %param.20) | copy-start | bytes 100
  7.2 59.7 %all-gather.5.cloned.1.call-start = ((), (), s32[]{:S(2)}) async-start(), calls=%async_computation | async-start | bytes 3276800 | tf_op jit(solution)/shard_map/all_gather | solution.py:106
  7.9 112.2 %copy-start.11 = (f32[2560]{0:T(1024)S(1)}, f32[2560]{0:T(1024)}, u32[]{:S(2)}) copy-start(f32[2560]{0:T(1024)} %param.14) | copy-start | bytes 30724
  7.9 112.2 %all-gather.7.cloned.1.call-start = ((), (), s32[]{:S(2)}) async-start(), calls=%async_computation.1 | async-start | bytes 8847360 | tf_op jit(solution)/shard_map/all_gather | solution.py:118
  12.4 151.8 %all-gather.9.cloned.1.call-start = ((), (), s32[]{:S(2)}) async-start(), calls=%async_computation.2 | async-start | bytes 2359296 | tf_op jit(solution)/shard_map/all_gather | solution.py:170
  69.2 62.9 %copy-start.8 = (f32[128]{0:T(128)S(1)}, f32[128]{0:T(128)}, u32[]{:S(2)}) copy-start(f32[128]{0:T(128)} %param.19) | copy-start | bytes 1540
  127.6 1.7 copy-start.3
  130.1 13.0 %copy-start.12 = (s32[32]{0:T(128)S(1)}, s32[32]{0:T(128)}, u32[]{:S(2)}) copy-start(s32[32]{0:T(128)} %param.21) | copy-start | bytes 388
  132.8 10.8 %copy-start.4 = (f32[512,1536]{1,0:T(8,128)S(1)}, f32[512,1536]{1,0:T(8,128)}, u32[]{:S(2)}) copy-start(f32[512,1536]{1,0:T(8,128)} %copy-done.3) | copy-start | bytes 9437188
  136.2 57.5 %all-gather.11.cloned.1.call-start = ((), (), s32[]{:S(2)}) async-start(), calls=%async_computation.3 | async-start | bytes 2359296 | tf_op jit(solution)/shard_map/all_gather | solution.py:171
  143.8 1.4 copy-start.9
  144.3 1.8 copy-start.5
  200.2 15.4 %copy-start.1 = (bf16[4096,256]{1,0:T(8,128)(2,1)S(1)}, bf16[4096,256]{1,0:T(8,128)(2,1)}, u32[]{:S(2)}) copy-start(bf16[4096,256]{1,0:T(8,128)(2,1)} %get-tuple-element.36) | copy-start | bytes 6291460 | tf_op jit(solution)/shard_map/cond
  259.0 15.4 %copy-start.2 = (bf16[4096,256]{1,0:T(8,128)(2,1)S(1)}, bf16[4096,256]{1,0:T(8,128)(2,1)}, u32[]{:S(2)}) copy-start(bf16[4096,256]{1,0:T(8,128)(2,1)} %get-tuple-element.43) | copy-start | bytes 6291460 | tf_op jit(solution)/shard_map/cond
  308.5 8.0 %copy-start = (bf16[4096,256]{1,0:T(8,128)(2,1)S(1)}, bf16[4096,256]{1,0:T(8,128)(2,1)}, u32[]{:S(2)}) copy-start(bf16[4096,256]{1,0:T(8,128)(2,1)} %all-gather.11.cloned.1.call-done) | copy-start | bytes 6291460
  310.7 8.9 %copy-start.6 = (bf16[256,1024]{1,0:T(8,128)(2,1)S(1)}, bf16[256,1024]{1,0:T(8,128)(2,1)}, u32[]{:S(2)}) copy-start(bf16[256,1024]{1,0:T(8,128)(2,1)} %convert_element_type.91) | copy-start | bytes 1572868
  311.8 7.7 %copy-start.7 = (bf16[256,1024]{1,0:T(8,128)(2,1)S(1)}, bf16[256,1024]{1,0:T(8,128)(2,1)}, u32[]{:S(2)}) copy-start(bf16[256,1024]{1,0:T(8,128)(2,1)} %convert_element_type.97) | copy-start | bytes 1572868
Sparse Core Ops, SparseCore 0:
  9.6 57.2 all-gather.4
  69.4 50.7 all-gather.6
  136.4 27.7 all-gather.8
  165.9 27.7 all-gather.10
where the time goes:
time: 329 us; the launch traced here: 328 us
  waiting for transfers between devices  146 us (44%)
  matrix products  78.8 us (24%)
  other arithmetic  52.8 us (16%)
  local copies, waits for them, and re-layouts  30.7 us (9%)
  between operations  19.1 us (6%)
    all_gather x1, waiting for transfers between devices, shards(): lax.all_gather(server_block, 'seq', axis=0, tiled=True)  50.9 us
    all_gather x1, waiting for transfers between devices, shards(): gathered = lax.all_gather(hidden, 'tp', axis=1, tiled=True)  49.7 us
    dot_general x2, matrix products, attend(): jnp.einsum('kgqn,nkd->kgqd', probs, value_piece.reshape(key_count, kv_hea...  34.9 us
    dot_general x2, matrix products, attend(): jnp.einsum('qkgd,nkd->kgqn', query_block.reshape(half_rows, kv_heads, gro...  30.8 us
    all_gather x1, waiting for transfers between devices, shards(): value_piece = lax.all_gather(values, 'seq', axis=0, tiled=True)  29.6 us
    reduce_sum x2, other arithmetic, attend(): denominator = jnp.sum(weights, axis=-1)  28.7 us
    all_gather x1, waiting for transfers between devices, shards(): key_piece = lax.all_gather(key_rows, 'seq', axis=0, tiled=True)  15.2 us
    reshape x2, local copies, waits for them, and re-layouts, attend(): key_piece.reshape(key_count, kv_heads, head_dim)  7.92 us
  transfers between devices with their start and end apart: 4, of which 4 were waited for; matrix products, arithmetic and copies ran while one was open for 6% of the time, Pallas kernels for 0%

commit v1 on v0

--- a/solution.py
+++ b/solution.py
@@ -167,8 +167,11 @@
     empty_pages = jnp.zeros((pages_dev, PAGE, key_cols), jnp.bfloat16)
     initial = (empty_state(), empty_state(), empty_pages, empty_pages)
     first_row = jnp.int32(0)
-    key_piece = lax.all_gather(key_rows, "seq", axis=0, tiled=True)
-    value_piece = lax.all_gather(values, "seq", axis=0, tiled=True)
+    key_piece, value_piece = jnp.split(
+        lax.all_gather(jnp.concatenate([key_rows, values], axis=1), "seq", axis=0, tiled=True),
+        [key_rows.shape[1]],
+        axis=1,
+    )
     key_count = key_piece.shape[0]
     key_slots = jnp.arange(key_count, dtype=jnp.int32)
     key_segments = segment_of(key_slots, prompt_ends)

time: 329 us -> 311 us (0.945)
  waiting for transfers between devices: 146 us -> 127 us
    all_gather x2 -> x1, waiting for transfers between devices: 44.8 us -> 25.9 us  [shards(): lax.all_gather(jnp.concatenate([key_rows, values], axis=1), 'seq', axis=0...]
    split x0 -> x1, local copies, waits for them, and re-layouts: none -> 3.81 us  [shards(): jnp.split(lax.all_gather(jnp.concatenate([key_rows, values], axis=1), 'se...]
  transfers between devices with their start and end apart: 4 -> 3, of which waited for: 4 -> 3; matrix products, arithmetic and copies ran while one was open for 6% -> 6% of each run, Pallas kernels for 0% -> 0%
where the time goes in v1:
time: 311 us; the launch traced here: 310 us
  waiting for transfers between devices  127 us (41%)
  matrix products  78.5 us (25%)
  other arithmetic  53.5 us (17%)
  local copies, waits for them, and re-layouts  31.1 us (10%)
  between operations  19.2 us (6%)
    all_gather x1, waiting for transfers between devices, shards(): lax.all_gather(server_block, 'seq', axis=0, tiled=True)  50.9 us
    all_gather x1, waiting for transfers between devices, shards(): gathered = lax.all_gather(hidden, 'tp', axis=1, tiled=True)  49.7 us
    dot_general x2, matrix products, attend(): jnp.einsum('kgqn,nkd->kgqd', probs, value_piece.reshape(key_count, kv_hea...  34.9 us
    dot_general x2, matrix products, attend(): jnp.einsum('qkgd,nkd->kgqn', query_block.reshape(half_rows, kv_heads, gro...  30.5 us
    reduce_sum x2, other arithmetic, attend(): denominator = jnp.sum(weights, axis=-1)  28.7 us
    all_gather x1, waiting for transfers between devices, shards(): lax.all_gather(jnp.concatenate([key_rows, values], axis=1), 'seq', axis=0...  25.9 us
    reshape x2, local copies, waits for them, and re-layouts, attend(): key_piece.reshape(key_count, kv_heads, head_dim)  8 us
    dot_general x1, matrix products, shards(): jnp.dot(normed, lax.all_gather(server_block, 'seq', axis=0, tiled=True),...  7.46 us
  transfers between devices with their start and end apart: 3, of which 3 were waited for; matrix products, arithmetic and copies ran while one was open for 6% of the time, Pallas kernels for 0%

profile of v1, /device:TPU:0, one launch (start us, length us, event | category | flops | bytes accessed | tf_op | source)
XLA Modules:
  0.0 309.9 jit_solution(6203004811738147577)
XLA Ops:
  15.5 1.8 multiply_cosine_fusion
  17.2 49.7 %all-gather.4.cloned.1.call-done = bf16[512,2560]{1,0:T(8,128)(2,1)} async-done(((bf16[512,640]{1,0:T(8,128)(2,1)}), bf16[512,2560]{1,0:T(8,128)(2,1)}) %all-gather.4.cloned.1.call-update) | async-done | bytes 2621456 | tf_op jit(solution)/shard_map/all_gather | solution.py:106
  66.9 2.3 fusion.26
  69.3 50.9 %all-gather.6.cloned.1.call-done = bf16[2560,1536]{1,0:T(8,128)(2,1)} async-done(((bf16[320,1536]{1,0:T(8,128)(2,1)}), bf16[2560,1536]{1,0:T(8,128)(2,1)}) %all-gather.6.cloned.1.call-update) | async-done | bytes 7864336 | tf_op jit(solution)/shard_map/all_gather | solution.py:118
  120.1 7.5 %fusion.29 = f32[512,1536]{1,0:T(8,128)S(1)} fusion(bf16[2560,1536]{1,0:T(8,128)(2,1)} %all-gather.6.cloned.1.call-done, bf16[512,2560]{1,0:T(8,128)(2,1)} %all-gather.4.cloned.1.call-done, f32[2560]{0:T(1024)S(1)} %copy-done.9, f32[512]{0:T(512)S(1)} %add_rsqrt_fusion.2), kind=kOutput, calls=%fused_computation.37 | convolution fusion | flops 4031774720 | bytes 13643776 | tf_op jit(solution)/shard_map/dot_general | solution.py:116
  127.6 1.6 copy-done
  131.7 1.9 subtract_convert_fusion.1
  146.1 25.9 %all-gather.8.cloned.1.call-done = bf16[4096,512]{1,0:T(8,128)(2,1)} async-done(((bf16[512,512]{1,0:T(8,128)(2,1)}), bf16[4096,512]{1,0:T(8,128)(2,1)}) %all-gather.8.cloned.1.call-update) | async-done | bytes 4194320 | tf_op jit(solution)/shard_map/all_gather | solution.py:171
  172.0 3.8 %fusion.59 = (bf16[4096,256]{1,0:T(8,128)(2,1)S(1)}, bf16[4096,256]{1,0:T(8,128)(2,1)}) fusion(bf16[4096,512]{1,0:T(8,128)(2,1)} %all-gather.8.cloned.1.call-done), kind=kLoop, calls=%fused_computation.97 | loop fusion | bytes 8388608 | tf_op jit(solution)/shard_map/split | solution.py:170
  175.8 55.6 %conditional.2 = (f32[2,4,256]{2,1,0:T(4,128)S(1)}, f32[2,4,256,128]{3,2,1,0:T(8,128)}) conditional(s32[]{:T(128)} %convert_element_type.81, () %tuple.24, (s32[4096]{0:T(1024)S(1)}, s32[256]{0:T(256)S(1)}, s32[4096]{0:T(1024)S(1)}, s32[256]{0:T(256)S(1)}, bf16[4096,256]{1,0:T(8,128)(2,1)}, /*index=5*/bf16[512,1024]{0,1:T(8,128)(2,1)}, ...), branch_computations={%region_9.10_spmd, %region_10.13_spmd} | conditional | flops 4390385664 | bytes 120145936 | solution.py:200
  177.2 4.0 %reshape.185 = bf16[4096,2,128]{2,1,0:T(2,128)(2,1)} reshape(bf16[4096,256]{1,0:T(8,128)(2,1)} %get-tuple-element.34) | data formatting | bytes 4194304 | tf_op jit(solution)/shard_map/cond/branch_1_fun/reshape | solution.py:62
  182.3 15.3 %fusion = (f32[2,4,256]{2,1,0:T(4,128)S(1)}, f32[2,4096,256,4]{2,1,3,0:T(8,128)}) fusion(pred[256,4096]{0,1:T(8,128)(4,1)S(1)} %compare_and_fusion, bf16[256,2,4,128]{0,3,2,1:T(8,128)(2,1)S(1)} %bitcast.86, bf16[4096,2,128,1]{2,1,0,3:T(2,128)(2,1)} %bitcast.80), kind=kOutput, calls=%fused_computation.2 | convolution fusion | flops 2172647424 | bytes 37232640 | tf_op jit(solution)/shard_map/cond/branch_1_fun/qkgd,nkd->kgqn/dot_general | solution.py:59
  197.6 2.1 reshape.187
  199.7 17.4 %fusion.5 = f32[2,4,256,128]{3,2,1,0:T(8,128)} fusion(f32[2,4096,256,4]{2,1,3,0:T(8,128)} %get-tuple-element.60, f32[2,4,256]{2,1,0:T(4,128)S(1)} %broadcast_maximum_fusion, pred[256,4096]{0,1:T(8,128)(4,1)S(1)} %compare_and_fusion, bf16[4096,2,128,1]{2,1,0,3:T(2,128)(2,1)} %bitcast.82), kind=kOutput, calls=%fused_computation.7 | convolution fusion | flops 2181038080 | bytes 37756928 | tf_op jit(solution)/shard_map/cond/branch_1_fun/kgqn,nkd->kgqd/dot_general | solution.py:73
  217.1 14.3 %fusion.4 = f32[2,4,256]{2,1,0:T(4,128)S(1)} fusion(f32[2,4096,256,4]{2,1,3,0:T(8,128)} %get-tuple-element.60, f32[2,4,256]{2,1,0:T(4,128)S(1)} %broadcast_maximum_fusion, pred[256,4096]{0,1:T(8,128)(4,1)S(1)} %compare_and_fusion), kind=kLoop, calls=%fused_computation.6 | loop fusion | flops 33552384 | bytes 34619392 | tf_op jit(solution)/shard_map/cond/branch_1_fun/reduce_sum | solution.py:71
  231.5 1.6 fusion.49
  234.6 55.9 %conditional.3 = (f32[2,4,256]{2,1,0:T(4,128)S(1)}, f32[2,4,256,128]{3,2,1,0:T(8,128)}) conditional(s32[]{:T(128)} %convert_element_type.94, () %tuple.26, (s32[4096]{0:T(1024)S(1)}, s32[256]{0:T(256)S(1)}, s32[4096]{0:T(1024)S(1)}, s32[256]{0:T(256)S(1)}, bf16[4096,256]{1,0:T(8,128)(2,1)}, /*index=5*/bf16[512,1024]{0,1:T(8,128)(2,1)}, ...), branch_computations={%region_15.16_spmd, %region_16.19_spmd} | conditional | flops 4390385664 | bytes 120145936 | solution.py:200
  236.0 4.0 %reshape.188 = bf16[4096,2,128]{2,1,0:T(2,128)(2,1)} reshape(bf16[4096,256]{1,0:T(8,128)(2,1)} %get-tuple-element.41) | data formatting | bytes 4194304 | tf_op jit(solution)/shard_map/cond/branch_1_fun/reshape | solution.py:62
  241.1 15.3 %fusion.13 = (f32[2,4,256]{2,1,0:T(4,128)S(1)}, f32[2,4096,256,4]{2,1,3,0:T(8,128)}) fusion(pred[256,4096]{0,1:T(8,128)(4,1)S(1)} %compare_and_fusion.1, bf16[256,2,4,128]{0,3,2,1:T(8,128)(2,1)S(1)} %bitcast.87, bf16[4096,2,128,1]{2,1,0,3:T(2,128)(2,1)} %bitcast.81), kind=kOutput, calls=%fused_computation.18 | convolution fusion | flops 2172647424 | bytes 37232640 | tf_op jit(solution)/shard_map/cond/branch_1_fun/qkgd,nkd->kgqn/dot_general | solution.py:59
  256.4 2.1 reshape.190
  258.5 17.4 %fusion.18 = f32[2,4,256,128]{3,2,1,0:T(8,128)} fusion(f32[2,4096,256,4]{2,1,3,0:T(8,128)} %get-tuple-element.62, f32[2,4,256]{2,1,0:T(4,128)S(1)} %broadcast_maximum_fusion.1, pred[256,4096]{0,1:T(8,128)(4,1)S(1)} %compare_and_fusion.1, bf16[4096,2,128,1]{2,1,0,3:T(2,128)(2,1)} %bitcast.83), kind=kOutput, calls=%fused_computation.23 | convolution fusion | flops 2181038080 | bytes 37756928 | tf_op jit(solution)/shard_map/cond/branch_1_fun/kgqn,nkd->kgqd/dot_general | solution.py:73
  275.9 14.3 %fusion.17 = f32[2,4,256]{2,1,0:T(4,128)S(1)} fusion(f32[2,4096,256,4]{2,1,3,0:T(8,128)} %get-tuple-element.62, f32[2,4,256]{2,1,0:T(4,128)S(1)} %broadcast_maximum_fusion.1, pred[256,4096]{0,1:T(8,128)(4,1)S(1)} %compare_and_fusion.1), kind=kLoop, calls=%fused_computation.22 | loop fusion | flops 33552384 | bytes 34619392 | tf_op jit(solution)/shard_map/cond/branch_1_fun/reduce_sum | solution.py:71
  293.7 3.6 %fusion.46 = bf16[4,128,256]{2,0,1:T(4,128)(2,1)} fusion(bf16[32,128,256]{2,1,0:T(8,128)(2,1)} %bitcast.77, pred[4]{0:T(512)(128)(4,1)S(1)} %fusion.52, s32[4]{0:T(128)S(1)} %select_reduce_fusion.1), kind=kOutput, calls=%fused_computation.52 | convolution fusion | flops 8650880 | bytes 2359316 | tf_op jit(solution)/shard_map/pj,jtc->ptc/dot_general | solution.py:206
  298.3 2.0 fusion.43
  (84 shorter events, 31.6 us)
Async XLA Ops:
  7.2 7.2 %copy-start.8 = (s32[8]{0:T(128)S(1)}, s32[8]{0:T(128)}, u32[]{:S(2)}) copy-start(s32[8]{0:T(128)} %param.20) | copy-start | bytes 100
  7.2 59.7 %all-gather.4.cloned.1.call-start = ((), (), s32[]{:S(2)}) async-start(), calls=%async_computation | async-start | bytes 3276800 | tf_op jit(solution)/shard_map/all_gather | solution.py:106
  7.9 112.2 %copy-start.9 = (f32[2560]{0:T(1024)S(1)}, f32[2560]{0:T(1024)}, u32[]{:S(2)}) copy-start(f32[2560]{0:T(1024)} %param.14) | copy-start | bytes 30724
  7.9 112.2 %all-gather.6.cloned.1.call-start = ((), (), s32[]{:S(2)}) async-start(), calls=%async_computation.1 | async-start | bytes 8847360 | tf_op jit(solution)/shard_map/all_gather | solution.py:118
  12.4 159.6 %all-gather.8.cloned.1.call-start = ((), (), s32[]{:S(2)}) async-start(), calls=%async_computation.2 | async-start | bytes 4718592 | tf_op jit(solution)/shard_map/all_gather | solution.py:171
  69.2 61.7 %copy-start.6 = (f32[128]{0:T(128)S(1)}, f32[128]{0:T(128)}, u32[]{:S(2)}) copy-start(f32[128]{0:T(128)} %param.19) | copy-start | bytes 1540
  127.6 1.7 copy-start
  130.0 10.2 %copy-start.10 = (s32[32]{0:T(128)S(1)}, s32[32]{0:T(128)}, u32[]{:S(2)}) copy-start(s32[32]{0:T(128)} %param.21) | copy-start | bytes 388
  130.3 4.1 %copy-start.5 = (bf16[512,256]{1,0:T(8,128)(2,1)S(1)}, bf16[512,256]{1,0:T(8,128)(2,1)}, u32[]{:S(2)}) copy-start(bf16[512,256]{1,0:T(8,128)(2,1)} %slice.80) | copy-start | bytes 786436
  131.7 9.0 %copy-start.1 = (f32[512,1536]{1,0:T(8,128)S(1)}, f32[512,1536]{1,0:T(8,128)}, u32[]{:S(2)}) copy-start(f32[512,1536]{1,0:T(8,128)} %copy-done) | copy-start | bytes 9437188
  140.9 1.4 copy-start.7
  141.4 1.8 copy-start.2
  292.1 9.3 %copy-start.3 = (bf16[256,1024]{1,0:T(8,128)(2,1)S(1)}, bf16[256,1024]{1,0:T(8,128)(2,1)}, u32[]{:S(2)}) copy-start(bf16[256,1024]{1,0:T(8,128)(2,1)} %convert_element_type.91) | copy-start | bytes 1572868
  293.7 7.7 %copy-start.4 = (bf16[256,1024]{1,0:T(8,128)(2,1)S(1)}, bf16[256,1024]{1,0:T(8,128)(2,1)}, u32[]{:S(2)}) copy-start(bf16[256,1024]{1,0:T(8,128)(2,1)} %convert_element_type.97) | copy-start | bytes 1572868
Sparse Core Ops, SparseCore 0:
  9.6 57.2 all-gather.3
  69.4 50.7 all-gather.5
  135.4 36.5 all-gather.7
